TPU v7x, 256 devices: a whole 4x4x8 slice. The times are simulated.
256 devices in a mesh: rep: 32 (over z, y_hi, core), fsdp: 8 (over x, y_lo).
Axes of the slice: x: 4, y: 4 (y_hi: 2, y_lo: 2; y = y_hi * 2 + y_lo), z: 8, core: 2. Of those that a mesh axis runs over, the one named last changes fastest.
Arguments:
- hidden: bfloat16 [32768, 7168], P(('rep', 'fsdp')), may hold values from -6 to 6
- grad_out: bfloat16 [32768, 4096], P(('rep', 'fsdp')), may hold values from -24 to 24
- down_weight: bfloat16 [7168, 4096], P('fsdp'), may hold values from -0.0625 to 0.0625
- hash_tiles: bfloat16 [3, 32, 7168], P(None, None, 'fsdp'), may hold values from -1 to 1, as said below
- momentum: float32 [8, 3, 32, 4096], P('fsdp', None, None, 'rep'), may hold values from -6 to 6
- error: float32 [8, 3, 32, 4096], P('fsdp', None, None, 'rep'), may hold values from -6 to 6
Outputs:
- grad_hidden: bfloat16 [32768, 7168], P(('rep', 'fsdp'))
- update: float32 [7168, 4096], P('fsdp', 'rep')
- new_momentum: float32 [8, 3, 32, 4096], P('fsdp', None, None, 'rep')
- new_error: float32 [8, 3, 32, 4096], P('fsdp', None, None, 'rep')
Inputs may be any that keep to these rules, and one draw needn't show every extreme that they name: `hash_tiles`: in every sketch row each hidden unit has exactly one nonzero entry, +1 or -1, in one of the 32 buckets; all other entries are 0.
All inputs are finite; a program needn't handle non-finite values.
Results may differ from a plain program's by a relative error of at most 0.0005.
Values may be sent and summed in bfloat16 or wider, within the bound.
No kernel may reach another device: no remote copies, remote signals or barrier semaphores. Data moves between devices by JAX's collectives and lax.ppermute only.
A program may use at most 128 MiB of HBM per device.

v0:
```python
import math
import jax
import jax.numpy as jnp
from jax import lax
from jax.sharding import PartitionSpec as P

momentum_decay = 0.9
step_size = 0.5


def split3(x):
    hi = lax.reduce_precision(x, exponent_bits=8, mantissa_bits=7)
    r1 = x - hi
    mid = lax.reduce_precision(r1, exponent_bits=8, mantissa_bits=7)
    lo = r1 - mid
    return jnp.stack([hi, mid, lo]).astype(jnp.bfloat16)


def grouped_scatter(blocks):
    me = lax.axis_index("rep")
    replicas = blocks.shape[0]
    inner = 4
    outer = replicas // inner
    rest = blocks.shape[1:]
    data = blocks.reshape((outer, inner) + rest)
    low = me % inner
    kept = lax.dynamic_index_in_dim(data, low, axis=1, keepdims=False)
    for mask in range(1, inner):
        send = lax.dynamic_index_in_dim(data, low ^ mask, axis=1, keepdims=False)
        kept = kept + lax.ppermute(send, "rep", [(j, j ^ mask) for j in range(replicas)])
    high = me // inner
    total = lax.dynamic_index_in_dim(kept, high, axis=0, keepdims=False)
    for mask in range(1, outer):
        send = lax.dynamic_index_in_dim(kept, high ^ mask, axis=0, keepdims=False)
        total = total + lax.ppermute(send, "rep", [(j, j ^ mask * inner) for j in range(replicas)])
    return total[None]


def on_device(hidden, grad_out, down_weight, hash_tiles, momentum, error):
    shards = lax.axis_size("fsdp")
    replicas = lax.axis_size("rep")
    tok_rows = grad_out.shape[0]
    model_width = grad_out.shape[1]
    shard_rows = down_weight.shape[0]
    rows_count = hash_tiles.shape[0]
    buckets = hash_tiles.shape[1]
    sketch_rows = rows_count * buckets
    columns = model_width // replicas
    total_tokens = tok_rows * shards * replicas
    table_scale = math.sqrt(buckets / (shard_rows * total_tokens))
    hash_float = hash_tiles.astype(jnp.float32)
    outgoing = jnp.concatenate(
        [
            jnp.broadcast_to(grad_out[None], (shards, tok_rows, model_width)),
            hidden.reshape(tok_rows, shards, shard_rows).transpose(1, 0, 2),
        ],
        axis=2,
    )
    arrived = lax.all_to_all(outgoing, "fsdp", split_axis=0, concat_axis=0, tiled=True)
    gathered = arrived[:, :, :model_width]
    hidden_cols = arrived[:, :, model_width:]
    partial_grads = jnp.einsum(
        "ptd,hd->tph", gathered, down_weight, preferred_element_type=jnp.float32
    ).astype(jnp.bfloat16)
    grad_hidden = lax.all_to_all(
        partial_grads, "fsdp", split_axis=1, concat_axis=1, tiled=True
    ).reshape(tok_rows, shards * shard_rows)
    projected = jnp.einsum(
        "ki,pti->kpt",
        hash_tiles.reshape(sketch_rows, shard_rows),
        hidden_cols,
        preferred_element_type=jnp.float32,
    ).reshape(sketch_rows, shards * tok_rows)
    pieces = split3(projected).reshape(3 * sketch_rows, shards * tok_rows)
    products = jnp.einsum(
        "mpt,ptd->md",
        pieces.reshape(3 * sketch_rows, shards, tok_rows),
        gathered,
        preferred_element_type=jnp.float32,
    ).reshape(3, sketch_rows, replicas, columns)
    summed = (products[0] + products[1] + products[2]).transpose(1, 0, 2)
    sketch_table = grouped_scatter(
        (summed * table_scale).reshape(replicas, rows_count, buckets, columns)
    )
    new_momentum = momentum_decay * momentum + sketch_table
    accumulated = error + step_size * new_momentum
    update = (
        jnp.einsum("jbi,jbc->ic", hash_float, accumulated[0], precision=lax.Precision.HIGHEST)
        / rows_count
    )
    encoded = jnp.einsum("jbi,ic->jbc", hash_float, update, precision=lax.Precision.HIGHEST)
    new_error = accumulated - encoded[None]
    return (grad_hidden, update, new_momentum, new_error)


def solution(mesh):
    return jax.shard_map(
        on_device,
        mesh=mesh,
        in_specs=(
            P(("rep", "fsdp"), None),
            P(("rep", "fsdp"), None),
            P("fsdp", None),
            P(None, None, "fsdp"),
            P("fsdp", None, None, "rep"),
            P("fsdp", None, None, "rep"),
        ),
        out_specs=(
            P(("rep", "fsdp"), None),
            P("fsdp", "rep"),
            P("fsdp", None, None, "rep"),
            P("fsdp", None, None, "rep"),
        ),
        check_vma=False,
    )
```

profile of v0, /device:TPU:1, one launch (start us, length us, event | category | flops | bytes accessed | tf_op | source)
XLA Modules:
  0.0 227.3 jit_solution(13042546810772492705)
XLA Ops:
  0.6 0.0 copy-start
  0.7 4.0 %copy.15 = bf16[128,7168]{0,1:T(8,128)(2,1)} copy(bf16[128,7168]{1,0:T(8,128)(2,1)} %param.6) | data formatting | bytes 3670016 | tf_op args[0]
  4.6 3.1 %copy.16 = bf16[128,8,896]{2,0,1:T(8,128)(2,1)S(1)} copy(bf16[128,8,896]{0,2,1:T(8,128)(2,1)} %bitcast.97) | data formatting | bytes 3670016 | tf_op jit(solution)/shard_map/reshape | solution.py:55
  7.7 1.0 broadcast_in_dim.12
  8.7 6.8 %pad_maximum_fusion = bf16[8,128,4992]{2,1,0:T(8,128)(2,1)} fusion(bf16[8,128,896]{2,1,0:T(8,128)(2,1)S(1)} %bitcast.95, bf16[8,128,4096]{2,1,0:T(8,128)(2,1)S(1)} %broadcast_in_dim.12), kind=kLoop, calls=%fused_computation | loop fusion | flops 20447232 | bytes 20447232 | tf_op jit(solution)/shard_map/concatenate | solution.py:52
  15.5 5.9 %all-to-all-start = ((bf16[8,128,4992]{2,1,0:T(8,128)(2,1)}), bf16[8,128,4992]{2,1,0:T(8,128)(2,1)}, u32[]{:S(2)}, u32[]{:S(2)}) async-start(bf16[8,128,4992]{2,1,0:T(8,128)(2,1)} %pad_maximum_fusion), calls=%async_computation | async-start | bytes 20447232 | tf_op jit(solution)/shard_map/all_to_all | solution.py:59
  21.4 139.0 %all-to-all-done = bf16[8,128,4992]{2,1,0:T(8,128)(2,1)} async-done(((bf16[8,128,4992]{2,1,0:T(8,128)(2,1)}), bf16[8,128,4992]{2,1,0:T(8,128)(2,1)}, u32[]{:S(2)}, u32[]{:S(2)}) %all-to-all-start) | async-done | bytes 10223648 | tf_op jit(solution)/shard_map/all_to_all | solution.py:59
  160.4 2.2 fusion.17
  162.5 0.2 copy.18
  162.8 0.1 reshape.73
  162.9 0.1 reduce-precision_convert_fusion.1
  163.0 0.1 pad_maximum_fusion.1
  163.0 0.1 copy.26
  163.1 5.0 %fusion.5 = f32[288,4096]{1,0:T(8,128)S(1)} fusion(bf16[8,128,4992]{2,1,0:T(8,128)(2,1)} %all-to-all-done, bf16[288,8,128]{2,1,0:T(8,128)(2,1)S(1)} %bitcast.101), kind=kOutput, calls=%fused_computation.6 | convolution fusion | flops 2415919104 | bytes 13697024 | tf_op jit(solution)/shard_map/mpt,ptd->md/dot_general | solution.py:75
  168.2 0.0 slice-start
  168.2 0.3 fusion.15
  168.5 0.0 slice-start.1
  168.5 0.3 copy.27
  168.7 1.8 constant_dynamic-slice_fusion.3
  170.5 0.1 copy.34
  170.6 5.3 %collective-permute-start.2 = (f32[8,3,32,128]{3,2,1,0:T(8,128)S(1)}, f32[8,3,32,128]{3,2,1,0:T(8,128)}, u32[]{:S(2)}, u32[]{:S(2)}) collective-permute-start(f32[8,3,32,128]{3,2,1,0:T(8,128)S(1)} %bitcast.102), channel_id=1, source_target_pairs={{0,24},{8,16},{16,8},{24,0},{32,56},{40,48},{48,40},{56,32},{64,88... | collective-permute-start | bytes 1179656 | tf_op jit(solution)/shard_map/ppermute | solution.py:30
  175.9 0.1 copy.35
  175.9 0.1 collective-permute-start.1
  176.1 0.8 copy.36
  176.9 0.4 collective-permute-start
  177.3 12.2 %convert_bitcast_fusion = bf16[128,8,896]{2,0,1:T(8,128)(2,1)} fusion(bf16[896,4096]{1,0:T(8,128)(2,1)S(1)} %bitcast.105, bf16[8,128,4992]{2,1,0:T(8,128)(2,1)} %all-to-all-done), kind=kOutput, calls=%fused_computation.9 | convolution fusion | flops 7517110272 | bytes 17563648 | tf_op jit(solution)/shard_map/ptd,hd->tph/dot_general | solution.py:62
  189.5 3.7 %all-to-all-start.1 = ((bf16[128,8,896]{2,0,1:T(8,128)(2,1)}), bf16[128,8,896]{2,0,1:T(8,128)(2,1)S(1)}, u32[]{:S(2)}, u32[]{:S(2)}) async-start(bf16[128,8,896]{2,0,1:T(8,128)(2,1)} %convert_bitcast_fusion), calls=%async_computation.1 | async-start | bytes 3670016 | tf_op jit(solution)/shard_map/all_to_all | solution.py:65
  193.3 0.5 collective-permute-done.1
  193.8 0.0 collective-permute-done
  193.8 1.4 fusion.25
  195.3 5.7 %collective-permute-start.9 = (f32[3,32,128]{2,1,0:T(8,128)S(1)}, f32[3,32,128]{2,1,0:T(8,128)S(1)}, u32[]{:S(2)}, u32[]{:S(2)}) collective-permute-start(f32[3,32,128]{2,1,0:T(8,128)S(1)} %get-tuple-element.17), channel_id=1, source_target_pairs={{0,224},{8,232},{16,240},{24,248},{32,192},{40,200},{48,208},{56,2... | collective-permute-start | bytes 147464 | tf_op jit(solution)/shard_map/ppermute | solution.py:35
  201.0 0.6 collective-permute-start.8
  201.5 3.5 %collective-permute-start.7 = (f32[3,32,128]{2,1,0:T(8,128)S(1)}, f32[3,32,128]{2,1,0:T(8,128)S(1)}, u32[]{:S(2)}, u32[]{:S(2)}) collective-permute-start(f32[3,32,128]{2,1,0:T(8,128)S(1)} %get-tuple-element.19), channel_id=1, source_target_pairs={{0,160},{8,168},{16,176},{24,184},{32,128},{40,136},{48,144},{56,1... | collective-permute-start | bytes 147464 | tf_op jit(solution)/shard_map/ppermute | solution.py:35
  205.0 1.8 collective-permute-start.6
  206.8 1.6 collective-permute-start.5
  208.4 0.0 collective-permute-done.9
  208.4 0.0 collective-permute-start.4
  208.5 1.9 collective-permute-start.3
  210.4 2.0 collective-permute-done.6
  212.4 0.0 collective-permute-done.5
  212.4 3.6 %collective-permute-done.4 = f32[3,32,128]{2,1,0:T(8,128)S(1)} collective-permute-done((f32[3,32,128]{2,1,0:T(8,128)S(1)}, f32[3,32,128]{2,1,0:T(8,128)S(1)}, u32[]{:S(2)}, u32[]{:S(2)}) %collective-permute-start.4) | collective-permute-done | bytes 49184 | tf_op jit(solution)/shard_map/ppermute | solution.py:35
  216.0 0.0 copy-start.2
  216.1 0.4 fusion.16
  216.5 1.0 copy.25
  217.4 1.0 fusion.20
  218.5 2.6 %all-to-all-done.1 = bf16[128,8,896]{2,0,1:T(8,128)(2,1)S(1)} async-done(((bf16[128,8,896]{2,0,1:T(8,128)(2,1)}), bf16[128,8,896]{2,0,1:T(8,128)(2,1)S(1)}, u32[]{:S(2)}, u32[]{:S(2)}) %all-to-all-start.1) | async-done | bytes 1835040 | tf_op jit(solution)/shard_map/all_to_all | solution.py:65
  221.1 2.4 %copy.17 = bf16[128,8,896]{0,2,1:T(8,128)(2,1)} copy(bf16[128,8,896]{2,0,1:T(8,128)(2,1)S(1)} %all-to-all-done.1) | data formatting | bytes 3670016 | tf_op jit(solution)/shard_map/all_to_all | solution.py:65
  223.5 3.9 %copy.24 = bf16[128,7168]{1,0:T(8,128)(2,1)} copy(bf16[128,7168]{0,1:T(8,128)(2,1)} %bitcast.96) | data formatting | bytes 3670016
  (17 shorter events, 0.1 us)
Async XLA Ops:
  0.6 159.7 %copy-start = (bf16[3,32,896]{2,1,0:T(8,128)(2,1)S(1)}, bf16[3,32,896]{2,1,0:T(8,128)(2,1)}, u32[]{:S(2)}) copy-start(bf16[3,32,896]{2,1,0:T(8,128)(2,1)} %param.9) | copy-start | bytes 516100
  0.6 7.0 %copy-start.1 = (bf16[128,4096]{1,0:T(8,128)(2,1)S(1)}, bf16[128,4096]{1,0:T(8,128)(2,1)}, u32[]{:S(2)}) copy-start(bf16[128,4096]{1,0:T(8,128)(2,1)} %param.7) | copy-start | bytes 3145732
  15.5 144.8 %all-to-all-start = ((bf16[8,128,4992]{2,1,0:T(8,128)(2,1)}), bf16[8,128,4992]{2,1,0:T(8,128)(2,1)}, u32[]{:S(2)}, u32[]{:S(2)}) async-start(bf16[8,128,4992]{2,1,0:T(8,128)(2,1)} %pad_maximum_fusion), calls=%async_computation | async-start | bytes 20447232 | tf_op jit(solution)/shard_map/all_to_all | solution.py:59
  168.2 9.1 %slice-start = ((s8[7340032]{0:T(1024)(128)(4,1)}), s8[4194304]{0:T(1024)(128)(4,1)S(1)}, s32[]{:S(2)}) async-start(s8[7340032]{0:T(1024)(128)(4,1)} %bitcast.104), calls=%async_computation.2 | async-start | bytes 8388608
  168.5 8.8 %slice-start.1 = ((s8[7340032]{0:T(1024)(128)(4,1)}), s8[3145728]{0:T(1024)(128)(4,1)S(1)}, s32[]{:S(2)}) async-start(s8[7340032]{0:T(1024)(128)(4,1)} %bitcast.104), calls=%async_computation.3 | async-start | bytes 6291456
  170.6 22.7 %collective-permute-start.2 = (f32[8,3,32,128]{3,2,1,0:T(8,128)S(1)}, f32[8,3,32,128]{3,2,1,0:T(8,128)}, u32[]{:S(2)}, u32[]{:S(2)}) collective-permute-start(f32[8,3,32,128]{3,2,1,0:T(8,128)S(1)} %bitcast.102), channel_id=1, source_target_pairs={{0,24},{8,16},{16,8},{24,0},{32,56},{40,48},{48,40},{56,32},{64,88... | collective-permute-start | bytes 1179656 | tf_op jit(solution)/shard_map/ppermute | solution.py:30
  175.9 17.9 %collective-permute-start.1 = (f32[8,3,32,128]{3,2,1,0:T(8,128)S(1)}, f32[8,3,32,128]{3,2,1,0:T(8,128)}, u32[]{:S(2)}, u32[]{:S(2)}) collective-permute-start(f32[8,3,32,128]{3,2,1,0:T(8,128)S(1)} %bitcast.103), channel_id=1, source_target_pairs={{0,16},{8,24},{16,0},{24,8},{32,48},{40,56},{48,32},{56,40},{64,80... | collective-permute-start | bytes 1179656 | tf_op jit(solution)/shard_map/ppermute | solution.py:30
  176.9 16.9 %collective-permute-start = (f32[8,3,32,128]{3,2,1,0:T(8,128)}, f32[8,3,32,128]{3,2,1,0:T(8,128)}, u32[]{:S(2)}, u32[]{:S(2)}) collective-permute-start(f32[8,3,32,128]{3,2,1,0:T(8,128)} %bitcast.93), channel_id=1, source_target_pairs={{0,8},{8,0},{16,24},{24,16},{32,40},{40,32},{48,56},{56,48},{64,72... | collective-permute-start | bytes 1179656 | tf_op jit(solution)/shard_map/ppermute | solution.py:30
  189.5 26.5 %copy-start.4 = (f32[1,3,32,128]{3,2,1,0:T(8,128)S(1)}, f32[1,3,32,128]{3,2,1,0:T(8,128)}, u32[]{:S(2)}) copy-start(f32[1,3,32,128]{3,2,1,0:T(8,128)} %param.10) | copy-start | bytes 147460
  189.5 26.6 %copy-start.3 = (f32[1,3,32,128]{3,2,1,0:T(8,128)S(1)}, f32[1,3,32,128]{3,2,1,0:T(8,128)}, u32[]{:S(2)}) copy-start(f32[1,3,32,128]{3,2,1,0:T(8,128)} %param.11) | copy-start | bytes 147460
  189.5 31.6 %all-to-all-start.1 = ((bf16[128,8,896]{2,0,1:T(8,128)(2,1)}), bf16[128,8,896]{2,0,1:T(8,128)(2,1)S(1)}, u32[]{:S(2)}, u32[]{:S(2)}) async-start(bf16[128,8,896]{2,0,1:T(8,128)(2,1)} %convert_bitcast_fusion), calls=%async_computation.1 | async-start | bytes 3670016 | tf_op jit(solution)/shard_map/all_to_all | solution.py:65
  195.3 13.2 %collective-permute-start.9 = (f32[3,32,128]{2,1,0:T(8,128)S(1)}, f32[3,32,128]{2,1,0:T(8,128)S(1)}, u32[]{:S(2)}, u32[]{:S(2)}) collective-permute-start(f32[3,32,128]{2,1,0:T(8,128)S(1)} %get-tuple-element.17), channel_id=1, source_target_pairs={{0,224},{8,232},{16,240},{24,248},{32,192},{40,200},{48,208},{56,2... | collective-permute-start | bytes 147464 | tf_op jit(solution)/shard_map/ppermute | solution.py:35
  201.0 7.5 %collective-permute-start.8 = (f32[3,32,128]{2,1,0:T(8,128)S(1)}, f32[3,32,128]{2,1,0:T(8,128)S(1)}, u32[]{:S(2)}, u32[]{:S(2)}) collective-permute-start(f32[3,32,128]{2,1,0:T(8,128)S(1)} %get-tuple-element.18), channel_id=1, source_target_pairs={{0,192},{8,200},{16,208},{24,216},{32,224},{40,232},{48,240},{56,2... | collective-permute-start | bytes 147464 | tf_op jit(solution)/shard_map/ppermute | solution.py:35
  201.5 8.8 %collective-permute-start.7 = (f32[3,32,128]{2,1,0:T(8,128)S(1)}, f32[3,32,128]{2,1,0:T(8,128)S(1)}, u32[]{:S(2)}, u32[]{:S(2)}) collective-permute-start(f32[3,32,128]{2,1,0:T(8,128)S(1)} %get-tuple-element.19), channel_id=1, source_target_pairs={{0,160},{8,168},{16,176},{24,184},{32,128},{40,136},{48,144},{56,1... | collective-permute-start | bytes 147464 | tf_op jit(solution)/shard_map/ppermute | solution.py:35
  205.0 7.4 %collective-permute-start.6 = (f32[3,32,128]{2,1,0:T(8,128)S(1)}, f32[3,32,128]{2,1,0:T(8,128)S(1)}, u32[]{:S(2)}, u32[]{:S(2)}) collective-permute-start(f32[3,32,128]{2,1,0:T(8,128)S(1)} %get-tuple-element.20), channel_id=1, source_target_pairs={{0,128},{8,136},{16,144},{24,152},{32,160},{40,168},{48,176},{56,1... | collective-permute-start | bytes 147464 | tf_op jit(solution)/shard_map/ppermute | solution.py:35
  206.8 5.6 %collective-permute-start.5 = (f32[3,32,128]{2,1,0:T(8,128)S(1)}, f32[3,32,128]{2,1,0:T(8,128)S(1)}, u32[]{:S(2)}, u32[]{:S(2)}) collective-permute-start(f32[3,32,128]{2,1,0:T(8,128)S(1)} %get-tuple-element.21), channel_id=1, source_target_pairs={{0,96},{8,104},{16,112},{24,120},{32,64},{40,72},{48,80},{56,88},{... | collective-permute-start | bytes 147464 | tf_op jit(solution)/shard_map/ppermute | solution.py:35
  208.4 7.5 %collective-permute-start.4 = (f32[3,32,128]{2,1,0:T(8,128)S(1)}, f32[3,32,128]{2,1,0:T(8,128)S(1)}, u32[]{:S(2)}, u32[]{:S(2)}) collective-permute-start(f32[3,32,128]{2,1,0:T(8,128)S(1)} %get-tuple-element.22), channel_id=1, source_target_pairs={{0,64},{8,72},{16,80},{24,88},{32,96},{40,104},{48,112},{56,120},{... | collective-permute-start | bytes 147464 | tf_op jit(solution)/shard_map/ppermute | solution.py:35
  208.5 7.5 %collective-permute-start.3 = (f32[3,32,128]{2,1,0:T(8,128)S(1)}, f32[3,32,128]{2,1,0:T(8,128)S(1)}, u32[]{:S(2)}, u32[]{:S(2)}) collective-permute-start(f32[3,32,128]{2,1,0:T(8,128)S(1)} %get-tuple-element.16), channel_id=1, source_target_pairs={{0,32},{8,40},{16,48},{24,56},{32,0},{40,8},{48,16},{56,24},{64,96... | collective-permute-start | bytes 147464 | tf_op jit(solution)/shard_map/ppermute | solution.py:35
  216.0 11.3 %copy-start.2 = (f32[1,3,32,128]{3,2,1,0:T(8,128)}, f32[1,3,32,128]{3,2,1,0:T(8,128)S(1)}, u32[]{:S(2)}) copy-start(f32[1,3,32,128]{3,2,1,0:T(8,128)S(1)} %bitcast_add_fusion.1) | copy-start | bytes 147460
where the time goes:
time: 228 us; the launch traced here: 227 us
  waiting for transfers between devices  148 us (65%)
  starting transfers between devices  30.4 us (13%)
  matrix products  20.8 us (9%)
  local copies, waits for them, and re-layouts  18.8 us (8%)
  other arithmetic  8.67 us (4%)
    all_to_all x1, waiting for transfers between devices, on_device(): lax.all_to_all(outgoing, 'fsdp', split_axis=0, concat_axis=0, tiled=True)  139 us
    ppermute x7, starting transfers between devices, grouped_scatter(): lax.ppermute(send, 'rep', [(j, j ^ mask * inner) for j in range(replicas)])  15.1 us
    dot_general x1, matrix products, on_device(): jnp.einsum('ptd,hd->tph', gathered, down_weight, preferred_element_type=j...  12.2 us
    unnamed x19, local copies, waits for them, and re-layouts  9.23 us
    concatenate x1, other arithmetic, on_device(): jnp.concatenate([jnp.broadcast_to(grad_out[None], (shards, tok_rows, mode...  6.79 us
    all_to_all x1, starting transfers between devices, on_device(): lax.all_to_all(outgoing, 'fsdp', split_axis=0, concat_axis=0, tiled=True)  5.86 us
    ppermute x3, starting transfers between devices, grouped_scatter(): lax.ppermute(send, 'rep', [(j, j ^ mask) for j in range(replicas)])  5.76 us
    ppermute x7, waiting for transfers between devices, grouped_scatter(): lax.ppermute(send, 'rep', [(j, j ^ mask * inner) for j in range(replicas)])  5.62 us
  transfers between devices with their start and end apart: 12, of which 5 were waited for; matrix products, arithmetic and copies ran while one was open for 7% of the time, Pallas kernels for 0%

commit v1 on v0

--- a/solution.py
+++ b/solution.py
@@ -62,8 +62,11 @@
     partial_grads = jnp.einsum(
         "ptd,hd->tph", gathered, down_weight, preferred_element_type=jnp.float32
     ).astype(jnp.bfloat16)
-    grad_hidden = lax.all_to_all(
-        partial_grads, "fsdp", split_axis=1, concat_axis=1, tiled=True
+    grad_hidden = jnp.concatenate(
+        lax.all_to_all(
+            jnp.stack(jnp.split(partial_grads, lax.axis_size("fsdp"), axis=1)), "fsdp", 0, 0
+        ),
+        axis=1,
     ).reshape(tok_rows, shards * shard_rows)
     projected = jnp.einsum(
         "ki,pti->kpt",

time: 228 us -> 258 us (1.13)
  waiting for transfers between devices: 148 us -> 171 us
  local copies, waits for them, and re-layouts: 18.8 us -> 24.4 us
    ppermute x3, waiting for transfers between devices: 0.54 us -> 26.9 us  [grouped_scatter(): lax.ppermute(send, 'rep', [(j, j ^ mask) for j in range(replicas)])]
    unnamed x19 -> x22, local copies, waits for them, and re-layouts: 9.23 us -> 14.1 us
  transfers between devices with their start and end apart: 12 -> 12, of which waited for: 5 -> 5; matrix products, arithmetic and copies ran while one was open for 7% -> 2% of each run, Pallas kernels for 0% -> 0%
where the time goes in v1:
time: 258 us; the launch traced here: 257 us
  waiting for transfers between devices  171 us (66%)
  starting transfers between devices  30.4 us (12%)
  local copies, waits for them, and re-layouts  24.4 us (9%)
  matrix products  22.1 us (9%)
  other arithmetic  8.81 us (3%)
    all_to_all x1, waiting for transfers between devices, on_device(): lax.all_to_all(outgoing, 'fsdp', split_axis=0, concat_axis=0, tiled=True)  139 us
    ppermute x3, waiting for transfers between devices, grouped_scatter(): lax.ppermute(send, 'rep', [(j, j ^ mask) for j in range(replicas)])  26.9 us
    ppermute x7, starting transfers between devices, grouped_scatter(): lax.ppermute(send, 'rep', [(j, j ^ mask * inner) for j in range(replicas)])  15.1 us
    unnamed x22, local copies, waits for them, and re-layouts  14.1 us
    dot_general x1, matrix products, on_device(): jnp.einsum('ptd,hd->tph', gathered, down_weight, preferred_element_type=j...  13.4 us
    concatenate x1, other arithmetic, on_device(): jnp.concatenate([jnp.broadcast_to(grad_out[None], (shards, tok_rows, mode...  6.93 us
    all_to_all x1, starting transfers between devices, on_device(): lax.all_to_all(outgoing, 'fsdp', split_axis=0, concat_axis=0, tiled=True)  5.86 us
    ppermute x3, starting transfers between devices, grouped_scatter(): lax.ppermute(send, 'rep', [(j, j ^ mask) for j in range(replicas)])  5.82 us
  transfers between devices with their start and end apart: 12, of which 5 were waited for; matrix products, arithmetic and copies ran while one was open for 2% of the time, Pallas kernels for 0%

profile of v1, /device:TPU:1, one launch (start us, length us, event | category | flops | bytes accessed | tf_op | source)
XLA Modules:
  0.0 257.4 jit_solution(14614801623805323550)
XLA Ops:
  0.6 3.9 %copy.15 = bf16[128,7168]{0,1:T(8,128)(2,1)} copy(bf16[128,7168]{1,0:T(8,128)(2,1)} %param.6) | data formatting | bytes 3670016 | tf_op args[0]
  4.6 3.1 %copy.16 = bf16[128,8,896]{2,0,1:T(8,128)(2,1)S(1)} copy(bf16[128,8,896]{0,2,1:T(8,128)(2,1)} %bitcast.131) | data formatting | bytes 3670016 | tf_op jit(solution)/shard_map/reshape | solution.py:55
  7.7 1.0 broadcast_in_dim.12
  8.8 6.9 %pad_maximum_fusion = bf16[8,128,4992]{2,1,0:T(8,128)(2,1)} fusion(bf16[8,128,896]{2,1,0:T(8,128)(2,1)S(1)} %bitcast.128, bf16[8,128,4096]{2,1,0:T(8,128)(2,1)S(1)} %broadcast_in_dim.12), kind=kLoop, calls=%fused_computation | loop fusion | flops 20447232 | bytes 20447232 | tf_op jit(solution)/shard_map/concatenate | solution.py:52
  15.7 5.9 %all-to-all-start = ((bf16[8,128,4992]{2,1,0:T(8,128)(2,1)}), bf16[8,128,4992]{2,1,0:T(8,128)(2,1)}, u32[]{:S(2)}, u32[]{:S(2)}) async-start(bf16[8,128,4992]{2,1,0:T(8,128)(2,1)} %pad_maximum_fusion), calls=%async_computation | async-start | bytes 20447232 | tf_op jit(solution)/shard_map/all_to_all | solution.py:59
  21.6 139.0 %all-to-all-done = bf16[8,128,4992]{2,1,0:T(8,128)(2,1)} async-done(((bf16[8,128,4992]{2,1,0:T(8,128)(2,1)}), bf16[8,128,4992]{2,1,0:T(8,128)(2,1)}, u32[]{:S(2)}, u32[]{:S(2)}) %all-to-all-start) | async-done | bytes 10223648 | tf_op jit(solution)/shard_map/all_to_all | solution.py:59
  160.5 13.4 %convert_bitcast_fusion = bf16[128,8,896]{2,0,1:T(8,128)(2,1)S(1)} fusion(bf16[896,4096]{1,0:T(8,128)(2,1)} %param.8, bf16[8,128,4992]{2,1,0:T(8,128)(2,1)} %all-to-all-done), kind=kOutput, calls=%fused_computation.9 | convolution fusion | flops 7517110272 | bytes 17563648 | tf_op jit(solution)/shard_map/ptd,hd->tph/dot_general | solution.py:62
  174.0 0.7 fusion.33
  174.7 0.7 fusion.32
  175.4 0.7 fusion.31
  176.1 0.7 fusion.30
  176.8 0.7 fusion.29
  177.5 0.7 fusion.28
  178.2 0.7 fusion.27
  178.9 2.2 fusion.17
  181.1 0.2 copy.18
  181.3 0.1 reshape.73
  181.4 0.1 reduce-precision_convert_fusion.1
  181.5 0.1 pad_maximum_fusion.1
  181.6 0.1 copy.26
  181.7 5.0 %fusion.5 = f32[288,4096]{1,0:T(8,128)S(1)} fusion(bf16[8,128,4992]{2,1,0:T(8,128)(2,1)} %all-to-all-done, bf16[288,8,128]{2,1,0:T(8,128)(2,1)S(1)} %bitcast.135), kind=kOutput, calls=%fused_computation.6 | convolution fusion | flops 2415919104 | bytes 13697024 | tf_op jit(solution)/shard_map/mpt,ptd->md/dot_general | solution.py:78
  186.7 0.3 fusion.15
  187.0 0.3 copy.27
  187.3 1.7 constant_dynamic-slice_fusion.3
  188.9 0.1 copy.34
  189.0 5.3 %collective-permute-start.2 = (f32[8,3,32,128]{3,2,1,0:T(8,128)S(1)}, f32[8,3,32,128]{3,2,1,0:T(8,128)}, u32[]{:S(2)}, u32[]{:S(2)}) collective-permute-start(f32[8,3,32,128]{3,2,1,0:T(8,128)S(1)} %bitcast.136), channel_id=1, source_target_pairs={{0,24},{8,16},{16,8},{24,0},{32,56},{40,48},{48,40},{56,32},{64,88... | collective-permute-start | bytes 1179656 | tf_op jit(solution)/shard_map/ppermute | solution.py:30
  194.3 0.1 copy.35
  194.4 0.1 collective-permute-start.1
  194.5 0.8 copy.36
  195.3 0.4 collective-permute-start
  195.7 0.7 fusion.26
  196.4 3.6 %all-to-all-start.1 = ((bf16[8,128,1,896]{3,1,2,0:T(8,128)(2,1)}), bf16[8,128,1,896]{3,1,2,0:T(8,128)(2,1)S(1)}, u32[]{:S(2)}, u32[]{:S(2)}) async-start(bf16[8,128,1,896]{3,1,2,0:T(8,128)(2,1)} %fusion.26), calls=%async_computation.1 | async-start | bytes 3670016 | tf_op jit(solution)/shard_map/all_to_all | solution.py:66
  200.1 12.9 %collective-permute-done.2 = f32[8,3,32,128]{3,2,1,0:T(8,128)} collective-permute-done((f32[8,3,32,128]{3,2,1,0:T(8,128)S(1)}, f32[8,3,32,128]{3,2,1,0:T(8,128)}, u32[]{:S(2)}, u32[]{:S(2)}) %collective-permute-start.2) | collective-permute-done | bytes 393248 | tf_op jit(solution)/shard_map/ppermute | solution.py:30
  213.0 13.9 %collective-permute-done.1 = f32[8,3,32,128]{3,2,1,0:T(8,128)} collective-permute-done((f32[8,3,32,128]{3,2,1,0:T(8,128)S(1)}, f32[8,3,32,128]{3,2,1,0:T(8,128)}, u32[]{:S(2)}, u32[]{:S(2)}) %collective-permute-start.1) | collective-permute-done | bytes 393248 | tf_op jit(solution)/shard_map/ppermute | solution.py:30
  227.0 1.4 fusion.25
  228.5 5.7 %collective-permute-start.9 = (f32[3,32,128]{2,1,0:T(8,128)S(1)}, f32[3,32,128]{2,1,0:T(8,128)S(1)}, u32[]{:S(2)}, u32[]{:S(2)}) collective-permute-start(f32[3,32,128]{2,1,0:T(8,128)S(1)} %get-tuple-element.17), channel_id=1, source_target_pairs={{0,224},{8,232},{16,240},{24,248},{32,192},{40,200},{48,208},{56,2... | collective-permute-start | bytes 147464 | tf_op jit(solution)/shard_map/ppermute | solution.py:35
  234.2 0.5 collective-permute-start.8
  234.7 3.5 %collective-permute-start.7 = (f32[3,32,128]{2,1,0:T(8,128)S(1)}, f32[3,32,128]{2,1,0:T(8,128)S(1)}, u32[]{:S(2)}, u32[]{:S(2)}) collective-permute-start(f32[3,32,128]{2,1,0:T(8,128)S(1)} %get-tuple-element.19), channel_id=1, source_target_pairs={{0,160},{8,168},{16,176},{24,184},{32,128},{40,136},{48,144},{56,1... | collective-permute-start | bytes 147464 | tf_op jit(solution)/shard_map/ppermute | solution.py:35
  238.2 1.8 collective-permute-start.6
  240.0 1.6 collective-permute-start.5
  241.7 1.9 collective-permute-start.3
  243.6 1.8 collective-permute-done.6
  245.4 3.2 %collective-permute-done.4 = f32[3,32,128]{2,1,0:T(8,128)S(1)} collective-permute-done((f32[3,32,128]{2,1,0:T(8,128)S(1)}, f32[3,32,128]{2,1,0:T(8,128)S(1)}, u32[]{:S(2)}, u32[]{:S(2)}) %collective-permute-start.4) | collective-permute-done | bytes 49184 | tf_op jit(solution)/shard_map/ppermute | solution.py:35
  248.7 0.4 fusion.16
  249.1 1.0 copy.25
  250.1 1.0 fusion.20
  251.1 2.4 copy.17
  253.5 3.9 %copy.24 = bf16[128,7168]{1,0:T(8,128)(2,1)} copy(bf16[128,7168]{0,1:T(8,128)(2,1)} %bitcast.130) | data formatting | bytes 3670016
  (20 shorter events, 0.1 us)
Async XLA Ops:
  0.6 178.3 %copy-start = (bf16[3,32,896]{2,1,0:T(8,128)(2,1)S(1)}, bf16[3,32,896]{2,1,0:T(8,128)(2,1)}, u32[]{:S(2)}) copy-start(bf16[3,32,896]{2,1,0:T(8,128)(2,1)} %param.9) | copy-start | bytes 516100
  4.6 3.2 %copy-start.1 = (bf16[128,4096]{1,0:T(8,128)(2,1)S(1)}, bf16[128,4096]{1,0:T(8,128)(2,1)}, u32[]{:S(2)}) copy-start(bf16[128,4096]{1,0:T(8,128)(2,1)} %param.7) | copy-start | bytes 3145732
  15.7 144.8 %all-to-all-start = ((bf16[8,128,4992]{2,1,0:T(8,128)(2,1)}), bf16[8,128,4992]{2,1,0:T(8,128)(2,1)}, u32[]{:S(2)}, u32[]{:S(2)}) async-start(bf16[8,128,4992]{2,1,0:T(8,128)(2,1)} %pad_maximum_fusion), calls=%async_computation | async-start | bytes 20447232 | tf_op jit(solution)/shard_map/all_to_all | solution.py:59
  189.0 24.0 %collective-permute-start.2 = (f32[8,3,32,128]{3,2,1,0:T(8,128)S(1)}, f32[8,3,32,128]{3,2,1,0:T(8,128)}, u32[]{:S(2)}, u32[]{:S(2)}) collective-permute-start(f32[8,3,32,128]{3,2,1,0:T(8,128)S(1)} %bitcast.136), channel_id=1, source_target_pairs={{0,24},{8,16},{16,8},{24,0},{32,56},{40,48},{48,40},{56,32},{64,88... | collective-permute-start | bytes 1179656 | tf_op jit(solution)/shard_map/ppermute | solution.py:30
  194.4 32.6 %collective-permute-start.1 = (f32[8,3,32,128]{3,2,1,0:T(8,128)S(1)}, f32[8,3,32,128]{3,2,1,0:T(8,128)}, u32[]{:S(2)}, u32[]{:S(2)}) collective-permute-start(f32[8,3,32,128]{3,2,1,0:T(8,128)S(1)} %bitcast.137), channel_id=1, source_target_pairs={{0,16},{8,24},{16,0},{24,8},{32,48},{40,56},{48,32},{56,40},{64,80... | collective-permute-start | bytes 1179656 | tf_op jit(solution)/shard_map/ppermute | solution.py:30
  195.3 31.7 %collective-permute-start = (f32[8,3,32,128]{3,2,1,0:T(8,128)}, f32[8,3,32,128]{3,2,1,0:T(8,128)}, u32[]{:S(2)}, u32[]{:S(2)}) collective-permute-start(f32[8,3,32,128]{3,2,1,0:T(8,128)} %bitcast.126), channel_id=1, source_target_pairs={{0,8},{8,0},{16,24},{24,16},{32,40},{40,32},{48,56},{56,48},{64,72... | collective-permute-start | bytes 1179656 | tf_op jit(solution)/shard_map/ppermute | solution.py:30
  196.4 54.7 %all-to-all-start.1 = ((bf16[8,128,1,896]{3,1,2,0:T(8,128)(2,1)}), bf16[8,128,1,896]{3,1,2,0:T(8,128)(2,1)S(1)}, u32[]{:S(2)}, u32[]{:S(2)}) async-start(bf16[8,128,1,896]{3,1,2,0:T(8,128)(2,1)} %fusion.26), calls=%async_computation.1 | async-start | bytes 3670016 | tf_op jit(solution)/shard_map/all_to_all | solution.py:66
  200.0 48.6 %copy-start.4 = (f32[1,3,32,128]{3,2,1,0:T(8,128)S(1)}, f32[1,3,32,128]{3,2,1,0:T(8,128)}, u32[]{:S(2)}) copy-start(f32[1,3,32,128]{3,2,1,0:T(8,128)} %param.10) | copy-start | bytes 147460
  200.1 48.6 %copy-start.3 = (f32[1,3,32,128]{3,2,1,0:T(8,128)S(1)}, f32[1,3,32,128]{3,2,1,0:T(8,128)}, u32[]{:S(2)}) copy-start(f32[1,3,32,128]{3,2,1,0:T(8,128)} %param.11) | copy-start | bytes 147460
  228.5 13.2 %collective-permute-start.9 = (f32[3,32,128]{2,1,0:T(8,128)S(1)}, f32[3,32,128]{2,1,0:T(8,128)S(1)}, u32[]{:S(2)}, u32[]{:S(2)}) collective-permute-start(f32[3,32,128]{2,1,0:T(8,128)S(1)} %get-tuple-element.17), channel_id=1, source_target_pairs={{0,224},{8,232},{16,240},{24,248},{32,192},{40,200},{48,208},{56,2... | collective-permute-start | bytes 147464 | tf_op jit(solution)/shard_map/ppermute | solution.py:35
  234.2 7.5 %collective-permute-start.8 = (f32[3,32,128]{2,1,0:T(8,128)S(1)}, f32[3,32,128]{2,1,0:T(8,128)S(1)}, u32[]{:S(2)}, u32[]{:S(2)}) collective-permute-start(f32[3,32,128]{2,1,0:T(8,128)S(1)} %get-tuple-element.18), channel_id=1, source_target_pairs={{0,192},{8,200},{16,208},{24,216},{32,224},{40,232},{48,240},{56,2... | collective-permute-start | bytes 147464 | tf_op jit(solution)/shard_map/ppermute | solution.py:35
  234.7 8.8 %collective-permute-start.7 = (f32[3,32,128]{2,1,0:T(8,128)S(1)}, f32[3,32,128]{2,1,0:T(8,128)S(1)}, u32[]{:S(2)}, u32[]{:S(2)}) collective-permute-start(f32[3,32,128]{2,1,0:T(8,128)S(1)} %get-tuple-element.19), channel_id=1, source_target_pairs={{0,160},{8,168},{16,176},{24,184},{32,128},{40,136},{48,144},{56,1... | collective-permute-start | bytes 147464 | tf_op jit(solution)/shard_map/ppermute | solution.py:35
  238.2 7.2 %collective-permute-start.6 = (f32[3,32,128]{2,1,0:T(8,128)S(1)}, f32[3,32,128]{2,1,0:T(8,128)S(1)}, u32[]{:S(2)}, u32[]{:S(2)}) collective-permute-start(f32[3,32,128]{2,1,0:T(8,128)S(1)} %get-tuple-element.20), channel_id=1, source_target_pairs={{0,128},{8,136},{16,144},{24,152},{32,160},{40,168},{48,176},{56,1... | collective-permute-start | bytes 147464 | tf_op jit(solution)/shard_map/ppermute | solution.py:35
  240.0 5.4 %collective-permute-start.5 = (f32[3,32,128]{2,1,0:T(8,128)S(1)}, f32[3,32,128]{2,1,0:T(8,128)S(1)}, u32[]{:S(2)}, u32[]{:S(2)}) collective-permute-start(f32[3,32,128]{2,1,0:T(8,128)S(1)} %get-tuple-element.21), channel_id=1, source_target_pairs={{0,96},{8,104},{16,112},{24,120},{32,64},{40,72},{48,80},{56,88},{... | collective-permute-start | bytes 147464 | tf_op jit(solution)/shard_map/ppermute | solution.py:35
  241.6 7.0 %collective-permute-start.4 = (f32[3,32,128]{2,1,0:T(8,128)S(1)}, f32[3,32,128]{2,1,0:T(8,128)S(1)}, u32[]{:S(2)}, u32[]{:S(2)}) collective-permute-start(f32[3,32,128]{2,1,0:T(8,128)S(1)} %get-tuple-element.22), channel_id=1, source_target_pairs={{0,64},{8,72},{16,80},{24,88},{32,96},{40,104},{48,112},{56,120},{... | collective-permute-start | bytes 147464 | tf_op jit(solution)/shard_map/ppermute | solution.py:35
  241.7 7.0 %collective-permute-start.3 = (f32[3,32,128]{2,1,0:T(8,128)S(1)}, f32[3,32,128]{2,1,0:T(8,128)S(1)}, u32[]{:S(2)}, u32[]{:S(2)}) collective-permute-start(f32[3,32,128]{2,1,0:T(8,128)S(1)} %get-tuple-element.16), channel_id=1, source_target_pairs={{0,32},{8,40},{16,48},{24,56},{32,0},{40,8},{48,16},{56,24},{64,96... | collective-permute-start | bytes 147464 | tf_op jit(solution)/shard_map/ppermute | solution.py:35
  248.7 4.9 %copy-start.2 = (f32[1,3,32,128]{3,2,1,0:T(8,128)}, f32[1,3,32,128]{3,2,1,0:T(8,128)S(1)}, u32[]{:S(2)}) copy-start(f32[1,3,32,128]{3,2,1,0:T(8,128)S(1)} %bitcast_add_fusion.1) | copy-start | bytes 147460
